TPU v7x, 512 devices: a whole 4x4x16 slice. The times are simulated.
512 devices in a mesh: seq: 128 (over z, x, core), fsdp: 4 (over y).
Axes of the slice: x: 4, y: 4, z: 16, core: 2. Of those that a mesh axis runs over, the one named last changes fastest.
Arguments:
- query_key: bfloat16 [131072, 3072], P(('seq', 'fsdp')), may hold values from -48 to 48
- values: bfloat16 [131072, 3072], P(('seq', 'fsdp')), may hold values from -6 to 6
- cluster_ids: int32 [24, 1024], replicated, may hold values from 0 to 127, as said below
Outputs:
- attended: bfloat16 [131072, 3072], P(('seq', 'fsdp'))
Inputs may be any that keep to these rules, and one draw needn't show every extreme that they name: `cluster_ids`: for every head and cluster at most 10 blocks name that cluster, and for every head some cluster is named by exactly 10 blocks. Among the (head, block) pairs of one group of 6 consecutive heads and one run of 8 blocks starting at a multiple of 8, no cluster is named more than 1 times, and some cluster exactly 1 times; the blocks of one such run name distinct clusters for each head.
All inputs are finite; a program needn't handle non-finite values.
Results may differ from a plain program's by a relative error of at most 0.0027.
Values may be sent and summed in bfloat16 or wider, within the bound.
No kernel may reach another device: no remote copies, remote signals or barrier semaphores. Data moves between devices by JAX's collectives and lax.ppermute only.
A program may use at most 64 MiB of HBM per device.

v0:
```python
import math
import jax
import jax.numpy as jnp
from jax import lax
from jax.sharding import PartitionSpec as P

BLK = 128
masked_score = -1e30


def by_index(source_table, row_index):
    padded = jnp.concatenate(
        [source_table, jnp.zeros((1,) + source_table.shape[1:], source_table.dtype)], axis=0
    )
    return padded[row_index]


def softmax_group(key_rows, positions, alive_rows, score_scale):
    half = BLK // 2
    blocks = key_rows.shape[0] // BLK

    def by_half(rows):
        shaped = rows.reshape((blocks, 2, half) + rows.shape[1:])
        return jnp.swapaxes(shaped, 0, 1).reshape(rows.shape)

    query_rows = by_half(key_rows)
    query_positions = by_half(positions)
    query_alive = by_half(alive_rows)
    scores = jnp.dot(query_rows, key_rows.T, preferred_element_type=jnp.float32) * score_scale
    allowed = alive_rows[None, :] & (positions[None, :] <= query_positions[:, None])
    scores = jnp.where(allowed, scores, masked_score)
    row_peak = jnp.max(scores, axis=1, keepdims=True)
    weights = jnp.where(allowed, jnp.exp(scores - row_peak), 0.0)
    row_total = jnp.where(query_alive[:, None], jnp.sum(weights, axis=1, keepdims=True), 1.0)
    weights = weights.astype(jnp.bfloat16).reshape(2, blocks * half, key_rows.shape[0])
    row_total = row_total.reshape(2, blocks * half, 1)
    return (weights[0], weights[1], row_total[0], row_total[1])


def shards(query_key, values, cluster_ids):
    seq_count = lax.axis_size("seq")
    group_count = lax.axis_size("fsdp")
    seq_index = lax.axis_index("seq")
    group_index = lax.axis_index("fsdp")
    heads_all = cluster_ids.shape[0]
    group_heads = heads_all // group_count
    head_dim = query_key.shape[1] // heads_all
    tok_rows = query_key.shape[0]
    shard_blocks = group_count * tok_rows // BLK
    all_blocks = cluster_ids.shape[1]
    item_count = group_heads * shard_blocks
    slot_count = max(1, item_count // seq_count)
    capacity = shard_blocks + min(shard_blocks // 4, seq_count - shard_blocks)
    group_rows = capacity * BLK
    send_rows = seq_count * slot_count
    score_scale = 1.0 / math.sqrt(head_dim)
    keys_local, values_local = (
        lax.all_to_all(query_key, "fsdp", split_axis=1, concat_axis=0, tiled=True),
        lax.all_to_all(values, "fsdp", split_axis=1, concat_axis=0, tiled=True),
    )

    def into_items(block_data):
        shaped = block_data.reshape(shard_blocks, BLK, group_heads, head_dim)
        return jnp.transpose(shaped, (2, 0, 1, 3)).reshape(item_count, BLK, head_dim)

    key_items = into_items(keys_local)
    value_items = into_items(values_local)
    group_ids = lax.dynamic_slice_in_dim(cluster_ids, group_index * group_heads, group_heads, 0)
    by_source = jnp.transpose(
        group_ids.reshape(group_heads, seq_count, shard_blocks), (1, 0, 2)
    ).reshape(seq_count, item_count)
    own_dest = lax.dynamic_index_in_dim(by_source, seq_index, 0, keepdims=False)
    item_ids = jnp.arange(item_count, dtype=jnp.int32)
    earlier = (own_dest[None, :] == own_dest[:, None]) & (item_ids[None, :] < item_ids[:, None])
    own_pos = own_dest * slot_count + jnp.sum(earlier.astype(jnp.int32), axis=1)
    row_ids = jnp.arange(send_rows, dtype=jnp.int32)
    slot_match = own_pos[None, :] == row_ids[:, None]
    send_pick = jnp.sum(jnp.where(slot_match, item_ids[None, :], 0), axis=1) + item_count * (
        1 - jnp.any(slot_match, axis=1).astype(jnp.int32)
    )
    received_mask = (by_source == seq_index).astype(jnp.int32)
    recv_pos = (
        jnp.arange(seq_count, dtype=jnp.int32)[:, None] * slot_count
        + jnp.cumsum(received_mask, axis=1)
        - received_mask
    )
    recv_by_head = jnp.transpose(
        recv_pos.reshape(seq_count, group_heads, shard_blocks), (1, 0, 2)
    ).reshape(group_heads * all_blocks)
    owned_mask = (group_ids == seq_index).astype(jnp.int32)
    ordinal = jnp.cumsum(owned_mask, axis=1) - owned_mask
    target = jnp.where(
        owned_mask > 0, jnp.arange(group_heads, dtype=jnp.int32)[:, None] * capacity + ordinal, -1
    ).reshape(group_heads * all_blocks)
    slot_ids = jnp.arange(group_heads * capacity, dtype=jnp.int32)
    matches = target[None, :] == slot_ids[:, None]
    present = jnp.any(matches, axis=1)
    source_row = jnp.sum(jnp.where(matches, recv_by_head[None, :], 0), axis=1) + send_rows * (
        1 - present.astype(jnp.int32)
    )
    block_ids = jnp.tile(jnp.arange(all_blocks, dtype=jnp.int32), group_heads)
    block_of = jnp.sum(jnp.where(matches, block_ids[None, :], 0), axis=1)
    arrived_k = lax.all_to_all(
        by_index(key_items, send_pick), "seq", split_axis=0, concat_axis=0, tiled=True
    )
    arrived_v = lax.all_to_all(
        by_index(value_items, send_pick), "seq", split_axis=0, concat_axis=0, tiled=True
    )
    key_grouped = by_index(arrived_k, source_row)
    value_grouped = by_index(arrived_v, source_row)
    positions = (block_of[:, None] * BLK + jnp.arange(BLK, dtype=jnp.int32)[None, :]).reshape(
        group_heads, group_rows
    )
    alive_rows = jnp.repeat(present, BLK).reshape(group_heads, group_rows)

    def one_head(operands):
        key_rows, where_at, alive_here = operands
        return softmax_group(key_rows, where_at, alive_here, score_scale)

    weights_0, weights_1, totals_0, totals_1 = lax.map(
        one_head, (key_grouped.reshape(group_heads, group_rows, head_dim), positions, alive_rows)
    )
    half = BLK // 2
    value_rows = value_grouped.reshape(group_heads, group_rows, head_dim)
    back_match = source_row[None, :] == row_ids[:, None]
    back_pick = jnp.sum(
        jnp.where(back_match, slot_ids[None, :], 0), axis=1
    ) + group_heads * capacity * (1 - jnp.any(back_match, axis=1).astype(jnp.int32))
    pieces = []
    for part in range(2):
        part_weights = (weights_0, weights_1)[part]
        weighted = jnp.einsum(
            "hqk,hkd->hqd", part_weights, value_rows, preferred_element_type=jnp.float32
        )
        part_total = (totals_0, totals_1)[part]
        outputs = (weighted / part_total).astype(jnp.bfloat16)
        outputs = outputs.reshape(group_heads * capacity, half, head_dim)
        returned = lax.all_to_all(
            by_index(outputs, back_pick), "seq", split_axis=0, concat_axis=0, tiled=True
        )
        own_output = by_index(returned, own_pos)
        token_major = jnp.transpose(
            own_output.reshape(group_heads, shard_blocks, half, head_dim), (1, 2, 0, 3)
        ).reshape(shard_blocks * half, group_heads * head_dim)
        pieces.append(lax.all_to_all(token_major, "fsdp", split_axis=0, concat_axis=1, tiled=True))
    own_blocks = tok_rows // BLK
    joined = jnp.stack(
        [piece.reshape(own_blocks, half, heads_all * head_dim) for piece in pieces], axis=1
    )
    return joined.reshape(tok_rows, heads_all * head_dim)


def solution(mesh):
    placed = (P(("seq", "fsdp"), None), P(("seq", "fsdp"), None), P())
    return jax.shard_map(
        shards, mesh=mesh, in_specs=placed, out_specs=P(("seq", "fsdp"), None), check_vma=False
    )
```

profile of v0, /device:TPU:32, one launch (start us, length us, event | category | flops | bytes accessed | tf_op | source)
XLA Modules:
  0.0 725.8 jit_solution(8790920589746454872)
XLA Ops:
  0.0 2.6 copy.104
  2.6 4.6 all-to-all-start
  20.4 7.5 %all-to-all-done = bf16[256,4,768]{0,2,1:T(8,128)(2,1)S(1)} async-done(((bf16[256,4,768]{0,2,1:T(8,128)(2,1)}), bf16[256,4,768]{0,2,1:T(8,128)(2,1)S(1)}, u32[]{:S(2)}, u32[]{:S(2)}) %all-to-all-start) | async-done | bytes 1572896 | tf_op jit(solution)/shard_map/all_to_all | solution.py:58
  27.9 3.6 all-to-all-start.2
  34.8 2.5 reshape.280
  40.7 3.1 gather_fusion
  43.8 7.5 %all-to-all-done.2 = bf16[256,4,768]{0,2,1:T(8,128)(2,1)S(1)} async-done(((bf16[256,4,768]{0,2,1:T(8,128)(2,1)}), bf16[256,4,768]{0,2,1:T(8,128)(2,1)S(1)}, u32[]{:S(2)}, u32[]{:S(2)}) %all-to-all-start.2) | async-done | bytes 1572896 | tf_op jit(solution)/shard_map/all_to_all | solution.py:59
  51.3 19.5 %all-to-all-start.1 = ((bf16[128,128,128]{2,1,0:T(8,128)(2,1)}), bf16[128,128,128]{2,1,0:T(8,128)(2,1)}, u32[]{:S(2)}, u32[]{:S(2)}) async-start(bf16[128,128,128]{2,1,0:T(8,128)(2,1)} %gather_fusion), calls=%async_computation.1 | async-start | bytes 8388608 | tf_op jit(solution)/shard_map/all_to_all | solution.py:103
  76.1 3.1 gather_fusion.2
  79.2 179.2 %all-to-all-done.1 = bf16[128,128,128]{2,1,0:T(8,128)(2,1)} async-done(((bf16[128,128,128]{2,1,0:T(8,128)(2,1)}), bf16[128,128,128]{2,1,0:T(8,128)(2,1)}, u32[]{:S(2)}, u32[]{:S(2)}) %all-to-all-start.1) | async-done | bytes 4194336 | tf_op jit(solution)/shard_map/all_to_all | solution.py:103
  258.4 9.4 %all-to-all-start.3 = ((bf16[128,128,128]{2,1,0:T(8,128)(2,1)}), bf16[128,128,128]{2,1,0:T(8,128)(2,1)}, u32[]{:S(2)}, u32[]{:S(2)}) async-start(bf16[128,128,128]{2,1,0:T(8,128)(2,1)} %gather_fusion.2), calls=%async_computation.3 | async-start | bytes 8388608 | tf_op jit(solution)/shard_map/all_to_all | solution.py:106
  268.3 5.8 concatenate.25
  274.1 3.1 gather_fusion.1
  277.3 41.2 %while.16 = (s32[]{:T(128)}, bf16[6,640,1280]{1,2,0:T(8,128)(2,1)}, bf16[6,640,1280]{1,2,0:T(8,128)(2,1)}, f32[6,640,1]{1,0,2:T(8,128)S(1)}, f32[6,640,1]{1,0,2:...) while((s32[]{:T(128)}, bf16[6,640,1280]{1,2,0:T(8,128)(2,1)}, ...), condition=%wide.region_12.13_spmd, body=%wide.region_9.12_spmd.sunk | while | flops 437451520 | bytes 25025912 | solution.py:120
  279.3 2.4 fusion.30
  286.2 2.4 fusion.30
  293.1 2.4 fusion.30
  299.9 2.4 fusion.30
  306.8 2.4 fusion.30
  318.5 137.1 %all-to-all-done.3 = bf16[128,128,128]{2,1,0:T(8,128)(2,1)} async-done(((bf16[128,128,128]{2,1,0:T(8,128)(2,1)}), bf16[128,128,128]{2,1,0:T(8,128)(2,1)}, u32[]{:S(2)}, u32[]{:S(2)}) %all-to-all-start.3) | async-done | bytes 4194336 | tf_op jit(solution)/shard_map/all_to_all | solution.py:106
  455.5 5.8 concatenate.27
  461.3 3.1 gather_fusion.3
  464.5 7.7 %divide_convert_fusion.1 = bf16[6,640,128]{2,1,0:T(8,128)(2,1)S(1)} fusion(f32[6,640]{1,0:T(8,128)S(1)} %bitcast.151, bf16[6,640,1280]{1,2,0:T(8,128)(2,1)} %get-tuple-element.50, bf16[6,1280,128]{2,1,0:T(8,128)(2,1)S(1)} %bitcast.140), kind=kOutput, calls=%fused_computation.26 | convolution fusion | flops 1259274240 | bytes 12794880 | tf_op jit(solution)/shard_map/hqk,hkd->hqd/dot_general | solution.py:132
  474.5 8.9 %all-to-all-start.4 = ((bf16[128,64,128]{2,1,0:T(8,128)(2,1)}), bf16[128,64,128]{2,1,0:T(8,128)(2,1)S(1)}, u32[]{:S(2)}, u32[]{:S(2)}) async-start(bf16[128,64,128]{2,1,0:T(8,128)(2,1)} %gather_fusion.4), calls=%async_computation.4 | async-start | bytes 4194304 | tf_op jit(solution)/shard_map/all_to_all | solution.py:138
  483.4 7.6 %divide_convert_fusion = bf16[6,640,128]{2,1,0:T(8,128)(2,1)S(1)} fusion(f32[6,640]{1,0:T(8,128)S(1)} %bitcast.152, bf16[6,640,1280]{1,2,0:T(8,128)(2,1)} %get-tuple-element.52, bf16[6,1280,128]{2,1,0:T(8,128)(2,1)} %bitcast.141), kind=kOutput, calls=%fused_computation.25 | convolution fusion | flops 1259274240 | bytes 12794880 | tf_op jit(solution)/shard_map/hqk,hkd->hqd/dot_general | solution.py:132
  493.2 88.5 %all-to-all-done.4 = bf16[128,64,128]{2,1,0:T(8,128)(2,1)S(1)} async-done(((bf16[128,64,128]{2,1,0:T(8,128)(2,1)}), bf16[128,64,128]{2,1,0:T(8,128)(2,1)S(1)}, u32[]{:S(2)}, u32[]{:S(2)}) %all-to-all-start.4) | async-done | bytes 2097184 | tf_op jit(solution)/shard_map/all_to_all | solution.py:138
  581.7 9.1 %all-to-all-start.6 = ((bf16[128,64,128]{2,1,0:T(8,128)(2,1)}), bf16[128,64,128]{2,1,0:T(8,128)(2,1)}, u32[]{:S(2)}, u32[]{:S(2)}) async-start(bf16[128,64,128]{2,1,0:T(8,128)(2,1)} %gather_fusion.6), calls=%async_computation.6 | async-start | bytes 4194304 | tf_op jit(solution)/shard_map/all_to_all | solution.py:138
  597.3 91.5 %all-to-all-done.6 = bf16[128,64,128]{2,1,0:T(8,128)(2,1)} async-done(((bf16[128,64,128]{2,1,0:T(8,128)(2,1)}), bf16[128,64,128]{2,1,0:T(8,128)(2,1)}, u32[]{:S(2)}, u32[]{:S(2)}) %all-to-all-start.6) | async-done | bytes 2097184 | tf_op jit(solution)/shard_map/all_to_all | solution.py:138
  688.8 4.2 all-to-all-start.5
  698.0 8.4 %all-to-all-done.5 = bf16[4,128,768]{2,1,0:T(8,128)(2,1)} async-done(((bf16[4,128,768]{2,1,0:T(8,128)(2,1)}), bf16[4,128,768]{2,1,0:T(8,128)(2,1)}, u32[]{:S(2)}, u32[]{:S(2)}) %all-to-all-start.5) | async-done | bytes 786464 | tf_op jit(solution)/shard_map/all_to_all | solution.py:145
  706.5 3.7 all-to-all-start.7
  712.5 10.5 %all-to-all-done.7 = bf16[4,128,768]{2,1,0:T(8,128)(2,1)S(1)} async-done(((bf16[4,128,768]{2,1,0:T(8,128)(2,1)}), bf16[4,128,768]{2,1,0:T(8,128)(2,1)S(1)}, u32[]{:S(2)}, u32[]{:S(2)}) %all-to-all-start.7) | async-done | bytes 786464 | tf_op jit(solution)/shard_map/all_to_all | solution.py:145
  (180 shorter events, 75.1 us)
Async XLA Ops:
  2.6 15.8 %copy-start.1 = (bf16[256,3072]{1,0:T(8,128)(2,1)S(1)}, bf16[256,3072]{1,0:T(8,128)(2,1)}, u32[]{:S(2)}) copy-start(bf16[256,3072]{1,0:T(8,128)(2,1)} %param.6) | copy-start | bytes 4718596
  2.6 25.3 %all-to-all-start = ((bf16[256,4,768]{0,2,1:T(8,128)(2,1)}), bf16[256,4,768]{0,2,1:T(8,128)(2,1)S(1)}, u32[]{:S(2)}, u32[]{:S(2)}) async-start(bf16[256,4,768]{0,2,1:T(8,128)(2,1)} %bitcast.13), calls=%async_computation | async-start | bytes 3145728 | tf_op jit(solution)/shard_map/all_to_all | solution.py:58
  17.1 2.9 copy-start.2
  17.1 3.1 copy-start.3
  20.0 11.5 %copy-start.4 = (s32[6144]{0:T(1024)S(1)}, s32[6144]{0:T(1024)}, u32[]{:S(2)}) copy-start(s32[6144]{0:T(1024)} %broadcast_in_dim.110) | copy-start | bytes 73732
  27.9 23.4 %all-to-all-start.2 = ((bf16[256,4,768]{0,2,1:T(8,128)(2,1)}), bf16[256,4,768]{0,2,1:T(8,128)(2,1)S(1)}, u32[]{:S(2)}, u32[]{:S(2)}) async-start(bf16[256,4,768]{0,2,1:T(8,128)(2,1)} %bitcast.132), calls=%async_computation.2 | async-start | bytes 3145728 | tf_op jit(solution)/shard_map/all_to_all | solution.py:59
  51.3 207.2 %all-to-all-start.1 = ((bf16[128,128,128]{2,1,0:T(8,128)(2,1)}), bf16[128,128,128]{2,1,0:T(8,128)(2,1)}, u32[]{:S(2)}, u32[]{:S(2)}) async-start(bf16[128,128,128]{2,1,0:T(8,128)(2,1)} %gather_fusion), calls=%async_computation.1 | async-start | bytes 8388608 | tf_op jit(solution)/shard_map/all_to_all | solution.py:103
  258.4 197.1 %all-to-all-start.3 = ((bf16[128,128,128]{2,1,0:T(8,128)(2,1)}), bf16[128,128,128]{2,1,0:T(8,128)(2,1)}, u32[]{:S(2)}, u32[]{:S(2)}) async-start(bf16[128,128,128]{2,1,0:T(8,128)(2,1)} %gather_fusion.2), calls=%async_computation.3 | async-start | bytes 8388608 | tf_op jit(solution)/shard_map/all_to_all | solution.py:106
  464.5 7.8 %copy-start = (bf16[60,128,128]{2,1,0:T(8,128)(2,1)}, bf16[60,128,128]{2,1,0:T(8,128)(2,1)S(1)}, u32[]{:S(2)}) copy-start(bf16[60,128,128]{2,1,0:T(8,128)(2,1)S(1)} %gather_fusion.3) | copy-start | bytes 5898244
  474.5 107.2 %all-to-all-start.4 = ((bf16[128,64,128]{2,1,0:T(8,128)(2,1)}), bf16[128,64,128]{2,1,0:T(8,128)(2,1)S(1)}, u32[]{:S(2)}, u32[]{:S(2)}) async-start(bf16[128,64,128]{2,1,0:T(8,128)(2,1)} %gather_fusion.4), calls=%async_computation.4 | async-start | bytes 4194304 | tf_op jit(solution)/shard_map/all_to_all | solution.py:138
  581.7 107.1 %all-to-all-start.6 = ((bf16[128,64,128]{2,1,0:T(8,128)(2,1)}), bf16[128,64,128]{2,1,0:T(8,128)(2,1)}, u32[]{:S(2)}, u32[]{:S(2)}) async-start(bf16[128,64,128]{2,1,0:T(8,128)(2,1)} %gather_fusion.6), calls=%async_computation.6 | async-start | bytes 4194304 | tf_op jit(solution)/shard_map/all_to_all | solution.py:138
  688.8 17.7 %all-to-all-start.5 = ((bf16[4,128,768]{2,1,0:T(8,128)(2,1)}), bf16[4,128,768]{2,1,0:T(8,128)(2,1)}, u32[]{:S(2)}, u32[]{:S(2)}) async-start(bf16[4,128,768]{2,1,0:T(8,128)(2,1)} %all_to_all.69), calls=%async_computation.5 | async-start | bytes 1572864 | tf_op jit(solution)/shard_map/all_to_all | solution.py:145
  706.5 16.5 %all-to-all-start.7 = ((bf16[4,128,768]{2,1,0:T(8,128)(2,1)}), bf16[4,128,768]{2,1,0:T(8,128)(2,1)S(1)}, u32[]{:S(2)}, u32[]{:S(2)}) async-start(bf16[4,128,768]{2,1,0:T(8,128)(2,1)} %all_to_all.73), calls=%async_computation.7 | async-start | bytes 1572864 | tf_op jit(solution)/shard_map/all_to_all | solution.py:145
where the time goes:
time: 735 us; the launch traced here: 726 us
  waiting for transfers between devices  530 us (72%)
  local copies, waits for them, and re-layouts  83.8 us (11%)
  starting transfers between devices  62.9 us (9%)
  matrix products  25.9 us (4%)
  other arithmetic  22 us (3%)
    all_to_all x2, waiting for transfers between devices, shards(): lax.all_to_all(by_index(outputs, back_pick), 'seq', split_axis=0, concat_...  180 us
    all_to_all x1, waiting for transfers between devices, shards(): lax.all_to_all(by_index(key_items, send_pick), 'seq', split_axis=0, conca...  179 us
    all_to_all x1, waiting for transfers between devices, shards(): lax.all_to_all(by_index(value_items, send_pick), 'seq', split_axis=0, con...  137 us
    gather x8, local copies, waits for them, and re-layouts, by_index(): return padded[row_index]  19.8 us
    all_to_all x1, starting transfers between devices, shards(): lax.all_to_all(by_index(key_items, send_pick), 'seq', split_axis=0, conca...  19.5 us
    all_to_all x2, waiting for transfers between devices, shards(): lax.all_to_all(token_major, 'fsdp', split_axis=0, concat_axis=1, tiled=True)  18.9 us
    concatenate x8, local copies, waits for them, and re-layouts, by_index(): jnp.concatenate([source_table, jnp.zeros((1,) + source_table.shape[1:], s...  18.7 us
    all_to_all x2, starting transfers between devices, shards(): lax.all_to_all(by_index(outputs, back_pick), 'seq', split_axis=0, concat_...  18 us
  transfers between devices with their start and end apart: 8, of which 8 were waited for; matrix products, arithmetic and copies ran while one was open for 14% of the time, Pallas kernels for 0%

commit v1 on v0

--- a/solution.py
+++ b/solution.py
@@ -6,6 +6,12 @@
 
 BLK = 128
 masked_score = -1e30
+
+
+def stacked_exchange(value, mesh_axis, split, join):
+    pieces = jnp.split(value, lax.axis_size(mesh_axis), axis=split)
+    arrived = lax.all_to_all(jnp.stack(pieces), mesh_axis, 0, 0)
+    return jnp.concatenate(arrived, axis=join)
 
 
 def by_index(source_table, row_index):
@@ -142,7 +148,7 @@
         token_major = jnp.transpose(
             own_output.reshape(group_heads, shard_blocks, half, head_dim), (1, 2, 0, 3)
         ).reshape(shard_blocks * half, group_heads * head_dim)
-        pieces.append(lax.all_to_all(token_major, "fsdp", split_axis=0, concat_axis=1, tiled=True))
+        pieces.append(stacked_exchange(token_major, "fsdp", 0, 1))
     own_blocks = tok_rows // BLK
     joined = jnp.stack(
         [piece.reshape(own_blocks, half, heads_all * head_dim) for piece in pieces], axis=1

time: 735 us -> 736 us (level)
  transfers between devices with their start and end apart: 8 -> 8, of which waited for: 8 -> 8; matrix products, arithmetic and copies ran while one was open for 14% -> 15% of each run, Pallas kernels for 0% -> 0%
where the time goes in v1:
time: 736 us; the launch traced here: 726 us
  waiting for transfers between devices  528 us (72%)
  local copies, waits for them, and re-layouts  85.5 us (12%)
  starting transfers between devices  61.7 us (8%)
  matrix products  25.9 us (4%)
  other arithmetic  24 us (3%)
    all_to_all x1, waiting for transfers between devices, shards(): lax.all_to_all(by_index(key_items, send_pick), 'seq', split_axis=0, conca...  179 us
    all_to_all x2, waiting for transfers between devices, shards(): lax.all_to_all(by_index(outputs, back_pick), 'seq', split_axis=0, concat_...  179 us
    all_to_all x1, waiting for transfers between devices, shards(): lax.all_to_all(by_index(value_items, send_pick), 'seq', split_axis=0, con...  137 us
    gather x8, local copies, waits for them, and re-layouts, by_index(): return padded[row_index]  21.4 us
    concatenate x8, local copies, waits for them, and re-layouts, by_index(): jnp.concatenate([source_table, jnp.zeros((1,) + source_table.shape[1:], s...  20 us
    all_to_all x1, starting transfers between devices, shards(): lax.all_to_all(by_index(key_items, send_pick), 'seq', split_axis=0, conca...  19.5 us
    all_to_all x2, waiting for transfers between devices, stacked_exchange(): arrived = lax.all_to_all(jnp.stack(pieces), mesh_axis, 0, 0)  18.3 us
    all_to_all x2, starting transfers between devices, shards(): lax.all_to_all(by_index(outputs, back_pick), 'seq', split_axis=0, concat_...  17.5 us
  transfers between devices with their start and end apart: 8, of which 8 were waited for; matrix products, arithmetic and copies ran while one was open for 15% of the time, Pallas kernels for 0%

profile of v1, /device:TPU:32, one launch (start us, length us, event | category | flops | bytes accessed | tf_op | source)
XLA Modules:
  0.0 726.3 jit_solution(9864927185608770934)
XLA Ops:
  0.0 2.6 copy.128
  2.6 4.6 all-to-all-start
  20.4 7.5 %all-to-all-done = bf16[256,4,768]{0,2,1:T(8,128)(2,1)S(1)} async-done(((bf16[256,4,768]{0,2,1:T(8,128)(2,1)}), bf16[256,4,768]{0,2,1:T(8,128)(2,1)S(1)}, u32[]{:S(2)}, u32[]{:S(2)}) %all-to-all-start) | async-done | bytes 1572896 | tf_op jit(solution)/shard_map/all_to_all | solution.py:64
  27.9 3.6 all-to-all-start.2
  34.8 2.5 reshape.292
  40.7 3.1 gather_fusion
  43.8 7.5 %all-to-all-done.2 = bf16[256,4,768]{0,2,1:T(8,128)(2,1)S(1)} async-done(((bf16[256,4,768]{0,2,1:T(8,128)(2,1)}), bf16[256,4,768]{0,2,1:T(8,128)(2,1)S(1)}, u32[]{:S(2)}, u32[]{:S(2)}) %all-to-all-start.2) | async-done | bytes 1572896 | tf_op jit(solution)/shard_map/all_to_all | solution.py:65
  51.3 19.5 %all-to-all-start.1 = ((bf16[128,128,128]{2,1,0:T(8,128)(2,1)}), bf16[128,128,128]{2,1,0:T(8,128)(2,1)}, u32[]{:S(2)}, u32[]{:S(2)}) async-start(bf16[128,128,128]{2,1,0:T(8,128)(2,1)} %gather_fusion), calls=%async_computation.1 | async-start | bytes 8388608 | tf_op jit(solution)/shard_map/all_to_all | solution.py:109
  76.1 3.1 gather_fusion.2
  79.2 179.2 %all-to-all-done.1 = bf16[128,128,128]{2,1,0:T(8,128)(2,1)} async-done(((bf16[128,128,128]{2,1,0:T(8,128)(2,1)}), bf16[128,128,128]{2,1,0:T(8,128)(2,1)}, u32[]{:S(2)}, u32[]{:S(2)}) %all-to-all-start.1) | async-done | bytes 4194336 | tf_op jit(solution)/shard_map/all_to_all | solution.py:109
  258.4 9.4 %all-to-all-start.3 = ((bf16[128,128,128]{2,1,0:T(8,128)(2,1)}), bf16[128,128,128]{2,1,0:T(8,128)(2,1)}, u32[]{:S(2)}, u32[]{:S(2)}) async-start(bf16[128,128,128]{2,1,0:T(8,128)(2,1)} %gather_fusion.2), calls=%async_computation.3 | async-start | bytes 8388608 | tf_op jit(solution)/shard_map/all_to_all | solution.py:112
  268.3 5.8 concatenate.25
  274.1 3.1 gather_fusion.1
  277.3 41.2 %while.16 = (s32[]{:T(128)}, bf16[6,640,1280]{1,2,0:T(8,128)(2,1)}, bf16[6,640,1280]{1,2,0:T(8,128)(2,1)}, f32[6,640,1]{1,0,2:T(8,128)S(1)}, f32[6,640,1]{1,0,2:...) while((s32[]{:T(128)}, bf16[6,640,1280]{1,2,0:T(8,128)(2,1)}, ...), condition=%wide.region_12.13_spmd, body=%wide.region_9.12_spmd.sunk | while | flops 437451520 | bytes 25025912 | solution.py:126
  279.3 2.4 fusion.32
  286.2 2.4 fusion.32
  293.1 2.4 fusion.32
  299.9 2.4 fusion.32
  318.5 137.1 %all-to-all-done.3 = bf16[128,128,128]{2,1,0:T(8,128)(2,1)} async-done(((bf16[128,128,128]{2,1,0:T(8,128)(2,1)}), bf16[128,128,128]{2,1,0:T(8,128)(2,1)}, u32[]{:S(2)}, u32[]{:S(2)}) %all-to-all-start.3) | async-done | bytes 4194336 | tf_op jit(solution)/shard_map/all_to_all | solution.py:112
  455.5 5.8 concatenate.27
  461.3 3.1 gather_fusion.3
  464.5 7.7 %divide_convert_fusion.1 = bf16[6,640,128]{2,1,0:T(8,128)(2,1)S(1)} fusion(f32[6,640]{1,0:T(8,128)S(1)} %bitcast.152, bf16[6,640,1280]{1,2,0:T(8,128)(2,1)} %get-tuple-element.50, bf16[6,1280,128]{2,1,0:T(8,128)(2,1)S(1)} %bitcast.141), kind=kOutput, calls=%fused_computation.26 | convolution fusion | flops 1259274240 | bytes 12794880 | tf_op jit(solution)/shard_map/hqk,hkd->hqd/dot_general | solution.py:138
  474.5 8.9 %all-to-all-start.4 = ((bf16[128,64,128]{2,1,0:T(8,128)(2,1)}), bf16[128,64,128]{2,1,0:T(8,128)(2,1)S(1)}, u32[]{:S(2)}, u32[]{:S(2)}) async-start(bf16[128,64,128]{2,1,0:T(8,128)(2,1)} %gather_fusion.4), calls=%async_computation.4 | async-start | bytes 4194304 | tf_op jit(solution)/shard_map/all_to_all | solution.py:144
  483.4 7.6 %divide_convert_fusion = bf16[6,640,128]{2,1,0:T(8,128)(2,1)S(1)} fusion(f32[6,640]{1,0:T(8,128)S(1)} %bitcast.153, bf16[6,640,1280]{1,2,0:T(8,128)(2,1)} %get-tuple-element.52, bf16[6,1280,128]{2,1,0:T(8,128)(2,1)} %bitcast.142), kind=kOutput, calls=%fused_computation.25 | convolution fusion | flops 1259274240 | bytes 12794880 | tf_op jit(solution)/shard_map/hqk,hkd->hqd/dot_general | solution.py:138
  493.2 88.5 %all-to-all-done.4 = bf16[128,64,128]{2,1,0:T(8,128)(2,1)S(1)} async-done(((bf16[128,64,128]{2,1,0:T(8,128)(2,1)}), bf16[128,64,128]{2,1,0:T(8,128)(2,1)S(1)}, u32[]{:S(2)}, u32[]{:S(2)}) %all-to-all-start.4) | async-done | bytes 2097184 | tf_op jit(solution)/shard_map/all_to_all | solution.py:144
  583.1 8.6 %all-to-all-start.6 = ((bf16[128,64,128]{2,1,0:T(8,128)(2,1)}), bf16[128,64,128]{2,1,0:T(8,128)(2,1)S(1)}, u32[]{:S(2)}, u32[]{:S(2)}) async-start(bf16[128,64,128]{2,1,0:T(8,128)(2,1)} %gather_fusion.6), calls=%async_computation.6 | async-start | bytes 4194304 | tf_op jit(solution)/shard_map/all_to_all | solution.py:144
  591.7 3.4 concatenate.29
  600.0 90.0 %all-to-all-done.6 = bf16[128,64,128]{2,1,0:T(8,128)(2,1)S(1)} async-done(((bf16[128,64,128]{2,1,0:T(8,128)(2,1)}), bf16[128,64,128]{2,1,0:T(8,128)(2,1)S(1)}, u32[]{:S(2)}, u32[]{:S(2)}) %all-to-all-start.6) | async-done | bytes 2097184 | tf_op jit(solution)/shard_map/all_to_all | solution.py:144
  690.0 3.5 all-to-all-start.5
  700.2 6.7 all-to-all-done.5
  706.9 3.7 all-to-all-start.7
  711.8 11.6 %all-to-all-done.7 = bf16[4,128,768]{2,1,0:T(8,128)(2,1)S(1)} async-done(((bf16[4,128,768]{2,1,0:T(8,128)(2,1)}), bf16[4,128,768]{2,1,0:T(8,128)(2,1)S(1)}, u32[]{:S(2)}, u32[]{:S(2)}) %all-to-all-start.7) | async-done | bytes 786464 | tf_op jit(solution)/shard_map/all_to_all | solution.py:13
  (198 shorter events, 77.8 us)
Async XLA Ops:
  2.6 15.8 %copy-start.2 = (bf16[256,3072]{1,0:T(8,128)(2,1)S(1)}, bf16[256,3072]{1,0:T(8,128)(2,1)}, u32[]{:S(2)}) copy-start(bf16[256,3072]{1,0:T(8,128)(2,1)} %param.6) | copy-start | bytes 4718596
  2.6 25.3 %all-to-all-start = ((bf16[256,4,768]{0,2,1:T(8,128)(2,1)}), bf16[256,4,768]{0,2,1:T(8,128)(2,1)S(1)}, u32[]{:S(2)}, u32[]{:S(2)}) async-start(bf16[256,4,768]{0,2,1:T(8,128)(2,1)} %bitcast.13), calls=%async_computation | async-start | bytes 3145728 | tf_op jit(solution)/shard_map/all_to_all | solution.py:64
  17.1 2.9 copy-start.3
  17.1 3.1 copy-start.4
  20.0 11.5 %copy-start.5 = (s32[6144]{0:T(1024)S(1)}, s32[6144]{0:T(1024)}, u32[]{:S(2)}) copy-start(s32[6144]{0:T(1024)} %broadcast_in_dim.110) | copy-start | bytes 73732
  27.9 23.4 %all-to-all-start.2 = ((bf16[256,4,768]{0,2,1:T(8,128)(2,1)}), bf16[256,4,768]{0,2,1:T(8,128)(2,1)S(1)}, u32[]{:S(2)}, u32[]{:S(2)}) async-start(bf16[256,4,768]{0,2,1:T(8,128)(2,1)} %bitcast.132), calls=%async_computation.2 | async-start | bytes 3145728 | tf_op jit(solution)/shard_map/all_to_all | solution.py:65
  51.3 207.2 %all-to-all-start.1 = ((bf16[128,128,128]{2,1,0:T(8,128)(2,1)}), bf16[128,128,128]{2,1,0:T(8,128)(2,1)}, u32[]{:S(2)}, u32[]{:S(2)}) async-start(bf16[128,128,128]{2,1,0:T(8,128)(2,1)} %gather_fusion), calls=%async_computation.1 | async-start | bytes 8388608 | tf_op jit(solution)/shard_map/all_to_all | solution.py:109
  258.4 197.1 %all-to-all-start.3 = ((bf16[128,128,128]{2,1,0:T(8,128)(2,1)}), bf16[128,128,128]{2,1,0:T(8,128)(2,1)}, u32[]{:S(2)}, u32[]{:S(2)}) async-start(bf16[128,128,128]{2,1,0:T(8,128)(2,1)} %gather_fusion.2), calls=%async_computation.3 | async-start | bytes 8388608 | tf_op jit(solution)/shard_map/all_to_all | solution.py:112
  464.5 7.8 %copy-start.1 = (bf16[60,128,128]{2,1,0:T(8,128)(2,1)}, bf16[60,128,128]{2,1,0:T(8,128)(2,1)S(1)}, u32[]{:S(2)}) copy-start(bf16[60,128,128]{2,1,0:T(8,128)(2,1)S(1)} %gather_fusion.3) | copy-start | bytes 5898244
  474.5 107.2 %all-to-all-start.4 = ((bf16[128,64,128]{2,1,0:T(8,128)(2,1)}), bf16[128,64,128]{2,1,0:T(8,128)(2,1)S(1)}, u32[]{:S(2)}, u32[]{:S(2)}) async-start(bf16[128,64,128]{2,1,0:T(8,128)(2,1)} %gather_fusion.4), calls=%async_computation.4 | async-start | bytes 4194304 | tf_op jit(solution)/shard_map/all_to_all | solution.py:144
  581.7 1.3 copy-start
  583.1 107.0 %all-to-all-start.6 = ((bf16[128,64,128]{2,1,0:T(8,128)(2,1)}), bf16[128,64,128]{2,1,0:T(8,128)(2,1)S(1)}, u32[]{:S(2)}, u32[]{:S(2)}) async-start(bf16[128,64,128]{2,1,0:T(8,128)(2,1)} %gather_fusion.6), calls=%async_computation.6 | async-start | bytes 4194304 | tf_op jit(solution)/shard_map/all_to_all | solution.py:144
  690.0 16.9 %all-to-all-start.5 = ((bf16[4,128,768]{2,1,0:T(8,128)(2,1)}), bf16[4,128,768]{2,1,0:T(8,128)(2,1)S(1)}, u32[]{:S(2)}, u32[]{:S(2)}) async-start(bf16[4,128,768]{2,1,0:T(8,128)(2,1)} %pad_maximum_fusion.1), calls=%async_computation.5 | async-start | bytes 1572864 | tf_op jit(solution)/shard_map/all_to_all | solution.py:13
  706.9 16.5 %all-to-all-start.7 = ((bf16[4,128,768]{2,1,0:T(8,128)(2,1)}), bf16[4,128,768]{2,1,0:T(8,128)(2,1)S(1)}, u32[]{:S(2)}, u32[]{:S(2)}) async-start(bf16[4,128,768]{2,1,0:T(8,128)(2,1)} %pad_maximum_fusion.2), calls=%async_computation.7 | async-start | bytes 1572864 | tf_op jit(solution)/shard_map/all_to_all | solution.py:13
